TPU v7x, 256 devices: a whole 4x4x8 slice. The times are simulated.
256 devices in a mesh: grp: 32 (over y, z_lo, core), tp: 8 (over x, z_hi).
Axes of the slice: x: 4, y: 4, z: 8 (z_hi: 2, z_lo: 4; z = z_hi * 4 + z_lo), core: 2. Of those that a mesh axis runs over, the one named last changes fastest.
Arguments:
- tok_ids: int32 [8192], P('grp'), may hold values from 0 to 16383
- accept: int32 [8192], P('grp'), may hold values 0 or 1
- sub_ids: int32 [8192], P('grp'), may hold values from 0 to 16383
- cache_len: int32 [32], replicated, may hold values from 256 to 3840, as said below
- spill: int32 [32], replicated, may hold values from 0 to 1792, as said below
- embed: bfloat16 [16384, 2048], P('grp', 'tp'), may hold values from -6 to 6
- attn_gain: float32 [2048], replicated, may hold values from 0.25 to 1.75
- w_query: bfloat16 [2048, 2048], P(None, 'tp'), may hold values from -0.125 to 0.125
- w_key: bfloat16 [2048, 512], P(None, 'tp'), as said below
- w_value: bfloat16 [2048, 512], P(None, 'tp'), as said below
- w_out: bfloat16 [2048, 2048], P('tp'), may hold values from -2.5 to 2.5
- mlp_gain: float32 [2048], replicated, may hold values from 0.25 to 1.75
- w_gate: bfloat16 [2048, 5632], P(None, 'tp'), may hold values from -0.125 to 0.125
- w_up: bfloat16 [2048, 5632], P(None, 'tp'), may hold values from -0.125 to 0.125
- w_down: bfloat16 [5632, 2048], P('tp'), may hold values from -0.078125 to 0.078125
- cache_keys: bfloat16 [65536, 512], P('grp', 'tp'), may hold values from -320 to 320, as said below
- cache_values: bfloat16 [65536, 512], P('grp', 'tp'), may hold values from -8 to 8, as said below
Outputs:
- first_out: bfloat16 [8192, 2048], P('grp', 'tp')
- second_out: bfloat16 [8192, 2048], P('grp', 'tp')
Inputs may be any that keep to these rules, and one draw needn't show every extreme that they name: Request g keeps cache_len[g] - spill[g] >= 256 positions in slots from 0 of store g and spill[g] positions in the last slots of store (g xor 1); for every g, cache_len[g] - spill[g] + spill[g xor 1] <= 2048. Of each pair of groups 2k, 2k + 1 at most one has spill above 0. `w_key`: the 2 stored copies of a key-value head are equal. `w_value`: the 2 stored copies of a key-value head are equal. `cache_keys`: the 2 stored copies of a key-value head are equal. `cache_values`: the 2 stored copies of a key-value head are equal.
All inputs are finite; a program needn't handle non-finite values. No bound on the sum of `accept` on one device may be relied on, other than what follows from the above.
Results may differ from a plain program's by a relative error of at most 0.024.
Values may be sent and summed in bfloat16 or wider, within the bound.
No kernel may reach another device: no remote copies, remote signals or barrier semaphores. Data moves between devices by JAX's collectives and lax.ppermute only.
A program may use at most 128 MiB of HBM per device.

v0:
```python
import jax
import jax.numpy as jnp
from jax import lax
from jax.sharding import PartitionSpec as P

HD = 64
EPSILON = 1e-05
SENTINEL = -1e30


def swapped(array, axis, bit):
    return lax.ppermute(array, axis, [(i, i ^ 1 << bit) for i in range(lax.axis_size(axis))])


def rms_normed(values, gain):
    square = jnp.mean(values * values, axis=-1, keepdims=True)
    return (values * lax.rsqrt(square + EPSILON) * gain).astype(jnp.bfloat16)


def rotate(vectors, positions):
    half = vectors.shape[-1] // 2
    exponent = jnp.arange(half, dtype=jnp.float32) * (-2.0 / vectors.shape[-1])
    freqs = jnp.power(jnp.float32(10000.0), exponent)
    angles = positions.astype(jnp.float32)[:, None] * freqs[None, :]
    cosine = jnp.cos(angles)[:, None, :]
    sine = jnp.sin(angles)[:, None, :]
    first = vectors[..., :half]
    second = vectors[..., half:]
    return jnp.concatenate(
        [first * cosine - second * sine, second * cosine + first * sine], axis=-1
    )


def partial_attention(query, keys, values, valid):
    scores = jnp.einsum("bcgd,kcd->bcgk", query, keys, preferred_element_type=jnp.float32) * 0.125
    scores = jnp.where(valid, scores, SENTINEL)
    top = jnp.max(scores, axis=-1)
    weights = jnp.where(valid, jnp.exp(scores - top[..., None]), 0.0)
    total = jnp.sum(weights, axis=-1)
    weighted = jnp.einsum(
        "bcgk,kcd->bcgd", weights.astype(jnp.bfloat16), values, preferred_element_type=jnp.float32
    )
    return (weighted, top, total)


def on_device(
    tok_ids,
    accept,
    sub_ids,
    cache_len,
    spill,
    embed,
    attn_gain,
    w_query,
    w_key,
    w_value,
    w_out,
    mlp_gain,
    w_gate,
    w_up,
    w_down,
    cache_keys,
    cache_values,
):
    block = tok_ids.shape[0]
    slots = cache_keys.shape[0]
    local_vocab = embed.shape[0]
    query_local = w_query.shape[1] // HD
    stored_local = w_key.shape[1] // HD
    per_stored = query_local // stored_local
    group_index = lax.axis_index("grp")
    shard_index = lax.axis_index("tp")
    own_count = cache_len[group_index] - spill[group_index]
    far_count = spill[group_index]
    positions = cache_len[group_index] + jnp.arange(block, dtype=jnp.int32)
    slot_ids = jnp.arange(slots, dtype=jnp.int32)
    tail_ids = slot_ids[block:]
    store_keys = cache_keys.reshape(slots, stored_local, HD)
    store_values = cache_values.reshape(slots, stored_local, HD)
    block_valid = jnp.ones((block,), dtype=bool)
    second_ids = jnp.where(accept == 1, sub_ids, tok_ids)
    vocab_base = group_index * local_vocab
    vocab_ids = jnp.arange(local_vocab, dtype=jnp.int32)

    def lookup(id_list):
        onehot = (id_list[:, None] - vocab_base == vocab_ids[None, :]).astype(jnp.bfloat16)
        return jnp.dot(onehot, embed, preferred_element_type=jnp.float32)

    all_first, all_second = (
        lax.all_gather(tok_ids, "grp", axis=0, tiled=True),
        lax.all_gather(second_ids, "grp", axis=0, tiled=True),
    )
    first_rows = lax.psum_scatter(
        lookup(all_first).astype(jnp.bfloat16), "grp", scatter_dimension=0, tiled=True
    )
    second_rows = lax.psum_scatter(
        lookup(all_second).astype(jnp.bfloat16), "grp", scatter_dimension=0, tiled=True
    )
    tail_keys, tail_values = swapped((cache_keys[block:], cache_values[block:]), "grp", 0)
    far_keys = tail_keys.reshape(slots - block, stored_local, HD)
    far_values = tail_values.reshape(slots - block, stored_local, HD)
    far_valid = tail_ids >= slots - far_count

    def denoise(x_part):
        width = x_part.shape[1]
        x_full = lax.all_gather(x_part, "tp", axis=1, tiled=True)
        normed = rms_normed(x_full.astype(jnp.float32), attn_gain)
        query = rotate(
            jnp.dot(normed, w_query, preferred_element_type=jnp.float32).reshape(
                block, query_local, HD
            ),
            positions,
        )
        query = query.astype(jnp.bfloat16).reshape(block, stored_local, per_stored, HD)
        new_keys = rotate(
            jnp.dot(normed, w_key, preferred_element_type=jnp.float32).reshape(
                block, stored_local, HD
            ),
            positions,
        ).astype(jnp.bfloat16)
        new_values = (
            jnp.dot(normed, w_value, preferred_element_type=jnp.float32)
            .reshape(block, stored_local, HD)
            .astype(jnp.bfloat16)
        )
        own_valid = slot_ids < own_count
        keys = jnp.concatenate([store_keys, far_keys, new_keys], axis=0)
        values = jnp.concatenate([store_values, far_values, new_values], axis=0)
        valid = jnp.concatenate([own_valid, far_valid, block_valid])
        weighted, top, total = partial_attention(query, keys, values, valid)
        attended = weighted / total[..., None]
        mixed = attended.reshape(block, query_local * HD).astype(jnp.bfloat16)
        head_term = jnp.dot(mixed, w_out, preferred_element_type=jnp.float32)
        head_sum = lax.psum(head_term.astype(jnp.bfloat16), "tp").astype(jnp.float32)
        resid_full = (x_full.astype(jnp.float32) + head_sum).astype(jnp.bfloat16)
        resid_part = lax.dynamic_slice_in_dim(resid_full, shard_index * width, width, 1)
        normed_mlp = rms_normed(resid_full.astype(jnp.float32), mlp_gain)
        gate = jnp.dot(normed_mlp, w_gate, preferred_element_type=jnp.float32)
        lift = jnp.dot(normed_mlp, w_up, preferred_element_type=jnp.float32)
        hidden = (jax.nn.silu(gate) * lift).astype(jnp.bfloat16)
        down_term = jnp.dot(hidden, w_down, preferred_element_type=jnp.float32)
        down_part = lax.psum_scatter(
            down_term.astype(jnp.bfloat16), "tp", scatter_dimension=1, tiled=True
        ).astype(jnp.float32)
        return (resid_part.astype(jnp.float32) + down_part).astype(jnp.bfloat16)

    return (denoise(first_rows), denoise(second_rows))


def solution(mesh):
    placed = (
        P("grp"),
        P("grp"),
        P("grp"),
        P(),
        P(),
        P("grp", "tp"),
        P(),
        P(None, "tp"),
        P(None, "tp"),
        P(None, "tp"),
        P("tp", None),
        P(),
        P(None, "tp"),
        P(None, "tp"),
        P("tp", None),
        P("grp", "tp"),
        P("grp", "tp"),
    )
    return jax.shard_map(
        on_device,
        mesh=mesh,
        in_specs=placed,
        out_specs=(P("grp", "tp"), P("grp", "tp")),
        check_vma=False,
    )
```

profile of v0, /device:TPU:8, one launch (start us, length us, event | category | flops | bytes accessed | tf_op | source)
XLA Modules:
  0.0 960.8 jit_solution(10995285730689573226)
XLA Ops:
  8.1 37.6 %all-gather.1 = s32[32,1,256]{2,1,0:T(1,128)S(1)} all-gather(s32[1,1,256]{2,1,0:T(1,128)S(1)} %bitcast.193), channel_id=1, replica_groups=mesh['grp'=32,'tp'=8] {'grp'}, dimensions={0}, use_global_device_ids=true | all-gather | bytes 33792 | tf_op jit(solution)/shard_map/all_gather | solution.py:91
  45.7 38.2 %all-gather = s32[32,1,256]{2,1,0:T(1,128)S(1)} all-gather(s32[1,1,256]{2,1,0:T(1,128)} %bitcast.192), channel_id=1, replica_groups=mesh['grp'=32,'tp'=8] {'grp'}, dimensions={0}, use_global_device_ids=true | all-gather | bytes 33792 | tf_op jit(solution)/shard_map/all_gather | solution.py:90
  83.9 6.3 fusion.10
  91.1 5.4 fusion.11
  96.6 131.9 %reduce-scatter.9.cloned.1.call-done = bf16[256,256]{1,0:T(8,128)(2,1)} async-done(((bf16[8192,256]{1,0:T(8,128)(2,1)}), bf16[256,256]{1,0:T(8,128)(2,1)}) %reduce-scatter.9.cloned.1.call-update) | async-done | bytes 131088 | tf_op jit(solution)/shard_map/reduce_scatter | solution.py:96
  228.6 151.1 %reduce-scatter.5.cloned.1.call-done = bf16[256,256]{1,0:T(8,128)(2,1)} async-done(((bf16[8192,256]{1,0:T(8,128)(2,1)}), bf16[256,256]{1,0:T(8,128)(2,1)}) %reduce-scatter.5.cloned.1.call-update) | async-done | bytes 131088 | tf_op jit(solution)/shard_map/reduce_scatter | solution.py:93
  380.5 1.6 slice.33
  386.7 73.9 %all-gather.7.cloned.1.call-done = bf16[256,2048]{1,0:T(8,128)(2,1)} async-done(((bf16[256,256]{1,0:T(8,128)(2,1)}), bf16[256,2048]{1,0:T(8,128)(2,1)}) %all-gather.7.cloned.1.call-update) | async-done | bytes 1048592 | tf_op jit(solution)/shard_map/all_gather | solution.py:106
  460.6 1.5 fusion.34
  462.1 58.2 %all-gather.5.cloned.1.call-done = bf16[256,2048]{1,0:T(8,128)(2,1)} async-done(((bf16[256,256]{1,0:T(8,128)(2,1)}), bf16[256,2048]{1,0:T(8,128)(2,1)}) %all-gather.5.cloned.1.call-update) | async-done | bytes 1048592 | tf_op jit(solution)/shard_map/all_gather | solution.py:106
  520.3 1.7 fusion.30
  522.0 2.3 fusion.114
  526.3 8.1 fusion.61
  534.5 14.5 %bitcast_reduce_fusion = (f32[256,4]{0,1:T(4,128)S(1)}, f32[256,4]{0,1:T(4,128)S(1)}, f32[4096,256,4]{1,0,2:T(8,128)}) fusion(pred[4096]{0:T(1024)(128)(4,1)S(1)} %pad_add_fusion, f32[4096,256,4]{1,0,2:T(8,128)} %fusion.61, bf16[256,4,32]{0,2,1:T(8,128)(2,1)S(1)} %get-tuple-element.13, bf16[256,4,32]{0,2,1:T(8,128)(2,1)S(1)} %get-tuple-element.12, ...), kind=kOutput, calls=%fused_computation.1 | convolution fusion | flops 564393984 | bytes 34222080 | tf_op jit(solution)/shard_map/bcgd,kcd->bcgk/dot_general | solution.py:35
  549.0 14.2 %fusion.8 = (f32[256,4]{0,1:T(4,128)S(1)}, f32[256,4]{0,1:T(4,128)S(1)}) fusion(f32[4096,256,4]{1,0,2:T(8,128)} %get-tuple-element.26, f32[256,4]{0,1:T(4,128)S(1)} %get-tuple-element.4, pred[4096]{0:T(1024)(128)(4,1)S(1)} %pad_add_fusion, f32[256,4]{0,1:T(4,128)S(1)} %get-tuple-element.5, f32[4096,256,4]{1,0,2:T(8,128)} %fusion.61), kind=kLoop, calls=%fused_computation.16 | loop fusion | flops 41940992 | bytes 33574912 | tf_op jit(solution)/shard_map/reduce_sum | solution.py:39
  563.8 5.4 fusion.51
  569.3 1.5 convolution_convert_fusion.3
  571.3 5.1 fusion.57
  576.4 1.5 convolution_convert_fusion.1
  578.2 190.4 %all-reduce.3.cloned.1.call-done = (bf16[256,2048]{1,0:T(8,128)(2,1)}, bf16[256,2048]{1,0:T(8,128)(2,1)}) async-done(((bf16[256,2048]{1,0:T(8,128)(2,1)}, bf16[256,2048]{1,0:T(8,128)(2,1)}), (bf16[256,2048]{1,0:T(8,128)(2,1)}, bf16[256,2048]{1,0:T(8,128)(2,1)})) %all-reduce.3.cloned.1.call-update) | async-done | bytes 2097168 | tf_op jit(solution)/shard_map/psum | solution.py:134
  768.6 2.2 fusion.24
  770.8 1.0 copy-done.4
  771.8 1.9 fusion.78
  773.8 6.6 convolution_convert_fusion.2
  780.5 2.2 fusion.27
  782.7 0.9 copy-done.5
  783.7 1.9 fusion.74
  785.6 6.6 convolution_convert_fusion
  792.3 72.7 %reduce-scatter.7.cloned.1.call-done = bf16[256,256]{1,0:T(8,128)(2,1)} async-done(((bf16[256,2048]{1,0:T(8,128)(2,1)}), bf16[256,256]{1,0:T(8,128)(2,1)}) %reduce-scatter.7.cloned.1.call-update) | async-done | bytes 131088 | tf_op jit(solution)/shard_map/reduce_scatter | solution.py:142
  865.0 1.7 add_convert_fusion.1
  866.6 85.6 %reduce-scatter.11.cloned.1.call-done = bf16[256,256]{1,0:T(8,128)(2,1)} async-done(((bf16[256,2048]{1,0:T(8,128)(2,1)}), bf16[256,256]{1,0:T(8,128)(2,1)}) %reduce-scatter.11.cloned.1.call-update) | async-done | bytes 131088 | tf_op jit(solution)/shard_map/reduce_scatter | solution.py:142
  952.3 1.7 add_convert_fusion
  (93 shorter events, 8.8 us)
Async XLA Ops:
  7.2 766.6 %copy-start = (bf16[704,2048]{1,0:T(8,128)(2,1)S(1)}, bf16[704,2048]{1,0:T(8,128)(2,1)}, u32[]{:S(2)}) copy-start(bf16[704,2048]{1,0:T(8,128)(2,1)} %param.31) | copy-start | bytes 8650756
  7.2 221.3 %reduce-scatter.9.cloned.1.call-start = ((), (), s32[]{:S(2)}) async-start(), calls=%async_computation.7 | async-start | bytes 4325376 | tf_op jit(solution)/shard_map/reduce_scatter | solution.py:96
  90.2 289.5 %reduce-scatter.5.cloned.1.call-start = ((), (), s32[]{:S(2)}) async-start(), calls=%async_computation.4 | async-start | bytes 4325376 | tf_op jit(solution)/shard_map/reduce_scatter | solution.py:93
  96.5 283.2 %copy-start.6 = (bf16[2048,64]{0,1:T(8,128)(2,1)S(1)}, bf16[2048,64]{0,1:T(8,128)(2,1)}, u32[]{:S(2)}) copy-start(bf16[2048,64]{0,1:T(8,128)(2,1)} %param.32) | copy-start | bytes 786436
  96.5 286.1 %copy-start.16 = (s32[32]{0:T(128)S(1)}, s32[32]{0:T(128)}, u32[]{:S(2)}) copy-start(s32[32]{0:T(128)} %param.20) | copy-start | bytes 388
  96.5 286.7 %copy-start.17 = (s32[32]{0:T(128)S(1)}, s32[32]{0:T(128)}, u32[]{:S(2)}) copy-start(s32[32]{0:T(128)} %param.21) | copy-start | bytes 388
  96.5 425.4 %copy-start.14 = (f32[2048]{0:T(1024)S(1)}, f32[2048]{0:T(1024)}, u32[]{:S(2)}) copy-start(f32[2048]{0:T(1024)} %param.23) | copy-start | bytes 24580
  96.6 364.0 %all-gather.7.cloned.1.call-start = ((), (), s32[]{:S(2)}) async-start(), calls=%async_computation.8 | async-start | bytes 1179648 | tf_op jit(solution)/shard_map/all_gather | solution.py:106
  228.5 291.7 %all-gather.5.cloned.1.call-start = ((), (), s32[]{:S(2)}) async-start(), calls=%async_computation.5 | async-start | bytes 1179648 | tf_op jit(solution)/shard_map/all_gather | solution.py:106
  379.7 388.9 %all-reduce.3.cloned.1.call-start = ((), (), s32[]{:S(2)}) async-start(), calls=%async_computation.10 | async-start | bytes 4194304 | tf_op jit(solution)/shard_map/psum | solution.py:134
  380.5 145.9 %collective-permute-start.1 = (bf16[1792,64]{0,1:T(8,128)(2,1)}, bf16[1792,64]{0,1:T(8,128)(2,1)S(1)}, u32[]{:S(2)}, u32[]{:S(2)}) collective-permute-start(bf16[1792,64]{0,1:T(8,128)(2,1)} %slice.35), channel_id=1, source_target_pairs={{0,8},{8,0},{16,24},{24,16},{32,40},{40,32},{48,56},{56,48},{64,72... | collective-permute-start | bytes 688136 | tf_op jit(solution)/shard_map/ppermute | solution.py:12
  382.1 181.6 %collective-permute-start = (bf16[1792,64]{0,1:T(8,128)(2,1)}, bf16[1792,64]{0,1:T(8,128)(2,1)}, u32[]{:S(2)}, u32[]{:S(2)}) collective-permute-start(bf16[1792,64]{0,1:T(8,128)(2,1)} %slice.33), channel_id=1, source_target_pairs={{0,8},{8,0},{16,24},{24,16},{32,40},{40,32},{48,56},{56,48},{64,72... | collective-permute-start | bytes 688136 | tf_op jit(solution)/shard_map/ppermute | solution.py:12
  520.3 4.0 copy-start.3
  520.3 4.0 copy-start.10
  521.9 3.1 copy-start.2
  521.9 3.1 copy-start.12
  534.5 29.3 %slice-start = ((s8[16777216]{0:T(1024)(128)(4,1)}), s8[4194304]{0:T(1024)(128)(4,1)S(1)}, s32[]{:S(2)}) async-start(s8[16777216]{0:T(1024)(128)(4,1)} %bitcast.174), calls=%async_computation.11 | async-start | bytes 8388608
  534.5 29.3 %slice-start.1 = ((s8[16777216]{0:T(1024)(128)(4,1)}), s8[4194304]{0:T(1024)(128)(4,1)S(1)}, s32[]{:S(2)}) async-start(s8[16777216]{0:T(1024)(128)(4,1)} %bitcast.174), calls=%async_computation.12 | async-start | bytes 8388608
  534.5 29.3 %slice-start.2 = ((s8[16777216]{0:T(1024)(128)(4,1)}), s8[4194304]{0:T(1024)(128)(4,1)S(1)}, s32[]{:S(2)}) async-start(s8[16777216]{0:T(1024)(128)(4,1)} %bitcast.174), calls=%async_computation.13 | async-start | bytes 8388608
  549.0 14.2 %copy-start.13 = (bf16[2048,64]{0,1:T(8,128)(2,1)S(1)}, bf16[2048,64]{0,1:T(8,128)(2,1)}, u32[]{:S(2)}) copy-start(bf16[2048,64]{0,1:T(8,128)(2,1)} %param.26) | copy-start | bytes 786436
  549.0 14.8 %slice-start.3 = ((s8[16777216]{0:T(1024)(128)(4,1)}), s8[4194304]{0:T(1024)(128)(4,1)S(1)}, s32[]{:S(2)}) async-start(s8[16777216]{0:T(1024)(128)(4,1)} %bitcast.174), calls=%async_computation.14 | async-start | bytes 8388608
  549.0 14.8 %copy-start.7 = (bf16[2048,64]{0,1:T(8,128)(2,1)S(1)}, bf16[2048,64]{0,1:T(8,128)(2,1)}, u32[]{:S(2)}) copy-start(bf16[2048,64]{0,1:T(8,128)(2,1)} %param.33) | copy-start | bytes 786436
  563.2 8.1 slice-start.4
  563.8 5.5 copy-start.1
  563.8 7.5 slice-start.5
  563.8 7.5 slice-start.6
  563.8 7.5 slice-start.7
  577.9 194.0 %copy-start.15 = (f32[2048]{0:T(1024)S(1)}, f32[2048]{0:T(1024)}, u32[]{:S(2)}) copy-start(f32[2048]{0:T(1024)} %param.28) | copy-start | bytes 24580
  577.9 287.1 %reduce-scatter.7.cloned.1.call-start = ((), (), s32[]{:S(2)}) async-start(), calls=%async_computation.6 | async-start | bytes 1179648 | tf_op jit(solution)/shard_map/reduce_scatter | solution.py:142
  768.6 3.2 copy-start.8
  780.5 171.8 %reduce-scatter.11.cloned.1.call-start = ((), (), s32[]{:S(2)}) async-start(), calls=%async_computation.9 | async-start | bytes 1179648 | tf_op jit(solution)/shard_map/reduce_scatter | solution.py:142
  780.5 3.2 copy-start.9
  (3 other events, 2.9 us)
Sparse Core Ops, SparseCore 0:
  90.3 138.1 reduce-scatter.8
  231.0 148.6 reduce-scatter.4
  382.2 78.3 all-gather.6
  462.9 57.3 all-gather.4
  578.0 190.5 all-reduce.2
  780.6 84.3 reduce-scatter.6
  869.4 82.7 reduce-scatter.10
where the time goes:
time: 961 us
  waiting for transfers between devices  764 us (80%)
  blocking collectives  75.8 us (8%)
  matrix products  70 us (7%)
  other arithmetic  27.1 us (3%)
  between operations  16.5 us (2%)
    psum x1, waiting for transfers between devices, denoise(): lax.psum(head_term.astype(jnp.bfloat16), 'tp').astype(jnp.float32)  190 us
    reduce_scatter x2, waiting for transfers between devices, denoise(): lax.psum_scatter(down_term.astype(jnp.bfloat16), 'tp', scatter_dimension=...  158 us
    reduce_scatter x1, waiting for transfers between devices, on_device(): lax.psum_scatter(lookup(all_first).astype(jnp.bfloat16), 'grp', scatter_d...  151 us
    all_gather x2, waiting for transfers between devices, denoise(): x_full = lax.all_gather(x_part, 'tp', axis=1, tiled=True)  132 us
    reduce_scatter x1, waiting for transfers between devices, on_device(): lax.psum_scatter(lookup(all_second).astype(jnp.bfloat16), 'grp', scatter_...  132 us
    all_gather x1, blocking collectives, on_device(): lax.all_gather(tok_ids, 'grp', axis=0, tiled=True)  38.2 us
    all_gather x1, blocking collectives, on_device(): lax.all_gather(second_ids, 'grp', axis=0, tiled=True)  37.6 us
    dot_general x2, matrix products, partial_attention(): jnp.einsum('bcgd,kcd->bcgk', query, keys, preferred_element_type=jnp.floa...  22.6 us
  transfers between devices with their start and end apart: 9, of which 7 were waited for; matrix products, arithmetic and copies ran while one was open for 7% of the time, Pallas kernels for 0%

commit v1 on v0

--- a/solution.py
+++ b/solution.py
@@ -131,7 +131,9 @@
         attended = weighted / total[..., None]
         mixed = attended.reshape(block, query_local * HD).astype(jnp.bfloat16)
         head_term = jnp.dot(mixed, w_out, preferred_element_type=jnp.float32)
-        head_sum = lax.psum(head_term.astype(jnp.bfloat16), "tp").astype(jnp.float32)
+        head_sum = jnp.sum(lax.all_gather(head_term.astype(jnp.bfloat16), "tp"), axis=0).astype(
+            jnp.float32
+        )
         resid_full = (x_full.astype(jnp.float32) + head_sum).astype(jnp.bfloat16)
         resid_part = lax.dynamic_slice_in_dim(resid_full, shard_index * width, width, 1)
         normed_mlp = rms_normed(resid_full.astype(jnp.float32), mlp_gain)

time: 961 us -> 1090 us (1.13)
  waiting for transfers between devices: 764 us -> 876 us
  other arithmetic: 27.1 us -> 39.8 us
    all_gather x0 -> x2, waiting for transfers between devices: none -> 309 us  [denoise(): lax.all_gather(head_term.astype(jnp.bfloat16), 'tp')]
    psum x1 -> x0, waiting for transfers between devices: 190 us -> none  [denoise(): lax.psum(head_term.astype(jnp.bfloat16), 'tp').astype(jnp.float32)]
    reduce_sum x0 -> x2, other arithmetic: none -> 12.9 us  [denoise(): jnp.sum(lax.all_gather(head_term.astype(jnp.bfloat16), 'tp'), axis=0)]
  transfers between devices with their start and end apart: 9 -> 10, of which waited for: 7 -> 8; matrix products, arithmetic and copies ran while one was open for 7% -> 9% of each run, Pallas kernels for 0% -> 0%
where the time goes in v1:
time: 1090 us
  waiting for transfers between devices  876 us (80%)
  blocking collectives  75.8 us (7%)
  matrix products  75 us (7%)
  other arithmetic  39.8 us (4%)
  between operations  16.4 us (2%)
    all_gather x2, waiting for transfers between devices, denoise(): lax.all_gather(head_term.astype(jnp.bfloat16), 'tp')  309 us
    reduce_scatter x2, waiting for transfers between devices, denoise(): lax.psum_scatter(down_term.astype(jnp.bfloat16), 'tp', scatter_dimension=...  153 us
    reduce_scatter x1, waiting for transfers between devices, on_device(): lax.psum_scatter(lookup(all_first).astype(jnp.bfloat16), 'grp', scatter_d...  152 us
    reduce_scatter x1, waiting for transfers between devices, on_device(): lax.psum_scatter(lookup(all_second).astype(jnp.bfloat16), 'grp', scatter_...  131 us
    all_gather x2, waiting for transfers between devices, denoise(): x_full = lax.all_gather(x_part, 'tp', axis=1, tiled=True)  131 us
    all_gather x1, blocking collectives, on_device(): lax.all_gather(tok_ids, 'grp', axis=0, tiled=True)  38.2 us
    all_gather x1, blocking collectives, on_device(): lax.all_gather(second_ids, 'grp', axis=0, tiled=True)  37.6 us
    dot_general x2, matrix products, partial_attention(): jnp.einsum('bcgd,kcd->bcgk', query, keys, preferred_element_type=jnp.floa...  22.8 us
  transfers between devices with their start and end apart: 10, of which 8 were waited for; matrix products, arithmetic and copies ran while one was open for 9% of the time, Pallas kernels for 0%

profile of v1, /device:TPU:8, one launch (start us, length us, event | category | flops | bytes accessed | tf_op | source)
XLA Modules:
  0.0 1090.7 jit_solution(7703473463430343621)
XLA Ops:
  8.1 37.6 %all-gather.3 = s32[32,1,256]{2,1,0:T(1,128)S(1)} all-gather(s32[1,1,256]{2,1,0:T(1,128)S(1)} %bitcast.195), channel_id=1, replica_groups=mesh['grp'=32,'tp'=8] {'grp'}, dimensions={0}, use_global_device_ids=true | all-gather | bytes 33792 | tf_op jit(solution)/shard_map/all_gather | solution.py:91
  45.7 38.2 %all-gather.2 = s32[32,1,256]{2,1,0:T(1,128)S(1)} all-gather(s32[1,1,256]{2,1,0:T(1,128)} %bitcast.194), channel_id=1, replica_groups=mesh['grp'=32,'tp'=8] {'grp'}, dimensions={0}, use_global_device_ids=true | all-gather | bytes 33792 | tf_op jit(solution)/shard_map/all_gather | solution.py:90
  83.9 6.3 fusion.10
  91.1 5.4 fusion.11
  96.6 131.5 %reduce-scatter.9.cloned.1.call-done = bf16[256,256]{1,0:T(8,128)(2,1)} async-done(((bf16[8192,256]{1,0:T(8,128)(2,1)}), bf16[256,256]{1,0:T(8,128)(2,1)}) %reduce-scatter.9.cloned.1.call-update) | async-done | bytes 131088 | tf_op jit(solution)/shard_map/reduce_scatter | solution.py:96
  228.2 151.9 %reduce-scatter.5.cloned.1.call-done = bf16[256,256]{1,0:T(8,128)(2,1)} async-done(((bf16[8192,256]{1,0:T(8,128)(2,1)}), bf16[256,256]{1,0:T(8,128)(2,1)}) %reduce-scatter.5.cloned.1.call-update) | async-done | bytes 131088 | tf_op jit(solution)/shard_map/reduce_scatter | solution.py:93
  380.9 1.6 slice.33
  387.1 72.8 %all-gather.11.cloned.1.call-done = bf16[256,2048]{1,0:T(8,128)(2,1)} async-done(((bf16[256,256]{1,0:T(8,128)(2,1)}), bf16[256,2048]{1,0:T(8,128)(2,1)}) %all-gather.11.cloned.1.call-update) | async-done | bytes 1048592 | tf_op jit(solution)/shard_map/all_gather | solution.py:106
  461.4 58.2 %all-gather.9.cloned.1.call-done = bf16[256,2048]{1,0:T(8,128)(2,1)} async-done(((bf16[256,256]{1,0:T(8,128)(2,1)}), bf16[256,2048]{1,0:T(8,128)(2,1)}) %all-gather.9.cloned.1.call-update) | async-done | bytes 1048592 | tf_op jit(solution)/shard_map/all_gather | solution.py:106
  519.6 1.7 fusion.30
  521.3 2.3 fusion.114
  525.7 8.1 fusion.61
  533.8 14.7 %bitcast_reduce_fusion = (f32[256,4]{0,1:T(4,128)S(1)}, f32[256,4]{0,1:T(4,128)S(1)}, f32[4096,256,4]{1,0,2:T(8,128)}) fusion(pred[4096]{0:T(1024)(128)(4,1)S(1)} %pad_add_fusion, f32[4096,256,4]{1,0,2:T(8,128)} %fusion.61, bf16[256,4,32]{0,2,1:T(8,128)(2,1)S(1)} %get-tuple-element.11, bf16[256,4,32]{0,2,1:T(8,128)(2,1)S(1)} %get-tuple-element.10, ...), kind=kOutput, calls=%fused_computation.1 | convolution fusion | flops 564393984 | bytes 34222080 | tf_op jit(solution)/shard_map/bcgd,kcd->bcgk/dot_general | solution.py:35
  548.5 14.0 %fusion.8 = (f32[256,4]{0,1:T(4,128)S(1)}, f32[256,4]{0,1:T(4,128)S(1)}) fusion(f32[4096,256,4]{1,0,2:T(8,128)} %get-tuple-element.24, f32[256,4]{0,1:T(4,128)S(1)} %get-tuple-element.4, pred[4096]{0:T(1024)(128)(4,1)S(1)} %pad_add_fusion, f32[256,4]{0,1:T(4,128)S(1)} %get-tuple-element.5, f32[4096,256,4]{1,0,2:T(8,128)} %fusion.61), kind=kLoop, calls=%fused_computation.16 | loop fusion | flops 41940992 | bytes 33574912 | tf_op jit(solution)/shard_map/reduce_sum | solution.py:39
  563.1 5.2 fusion.51
  568.3 1.5 convolution_convert_fusion.3
  569.9 1.7 fusion.47
  571.6 8.9 fusion.57
  582.2 156.9 %all-gather.13.cloned.1.call-done = bf16[2048,2048]{1,0:T(8,128)(2,1)} async-done(((bf16[256,2048]{1,0:T(8,128)(2,1)}), bf16[2048,2048]{1,0:T(8,128)(2,1)}) %all-gather.13.cloned.1.call-update) | async-done | bytes 8388624 | tf_op jit(solution)/shard_map/all_gather | solution.py:134
  739.2 6.5 reduce_sum.80
  745.6 2.2 fusion.24
  748.9 2.0 fusion.78
  750.9 6.7 convolution_convert_fusion.2
  757.9 151.7 %all-gather.15.cloned.1.call-done = bf16[2048,2048]{1,0:T(8,128)(2,1)} async-done(((bf16[256,2048]{1,0:T(8,128)(2,1)}), bf16[2048,2048]{1,0:T(8,128)(2,1)}) %all-gather.15.cloned.1.call-update) | async-done | bytes 8388624 | tf_op jit(solution)/shard_map/all_gather | solution.py:134
  909.7 6.4 reduce_sum.84
  916.0 2.2 fusion.27
  919.2 2.0 fusion.74
  921.2 6.6 convolution_convert_fusion
  927.9 67.1 %reduce-scatter.7.cloned.1.call-done = bf16[256,256]{1,0:T(8,128)(2,1)} async-done(((bf16[256,2048]{1,0:T(8,128)(2,1)}), bf16[256,256]{1,0:T(8,128)(2,1)}) %reduce-scatter.7.cloned.1.call-update) | async-done | bytes 131088 | tf_op jit(solution)/shard_map/reduce_scatter | solution.py:144
  995.0 1.7 add_convert_fusion.1
  996.6 85.6 %reduce-scatter.11.cloned.1.call-done = bf16[256,256]{1,0:T(8,128)(2,1)} async-done(((bf16[256,2048]{1,0:T(8,128)(2,1)}), bf16[256,256]{1,0:T(8,128)(2,1)}) %reduce-scatter.11.cloned.1.call-update) | async-done | bytes 131088 | tf_op jit(solution)/shard_map/reduce_scatter | solution.py:144
  1082.2 1.7 add_convert_fusion
  (91 shorter events, 13.5 us)
Async XLA Ops:
  7.2 743.7 %copy-start = (bf16[704,2048]{1,0:T(8,128)(2,1)S(1)}, bf16[704,2048]{1,0:T(8,128)(2,1)}, u32[]{:S(2)}) copy-start(bf16[704,2048]{1,0:T(8,128)(2,1)} %param.31) | copy-start | bytes 8650756
  7.2 220.9 %reduce-scatter.9.cloned.1.call-start = ((), (), s32[]{:S(2)}) async-start(), calls=%async_computation.7 | async-start | bytes 4325376 | tf_op jit(solution)/shard_map/reduce_scatter | solution.py:96
  90.2 289.9 %reduce-scatter.5.cloned.1.call-start = ((), (), s32[]{:S(2)}) async-start(), calls=%async_computation.4 | async-start | bytes 4325376 | tf_op jit(solution)/shard_map/reduce_scatter | solution.py:93
  96.5 283.6 %copy-start.7 = (bf16[2048,64]{0,1:T(8,128)(2,1)S(1)}, bf16[2048,64]{0,1:T(8,128)(2,1)}, u32[]{:S(2)}) copy-start(bf16[2048,64]{0,1:T(8,128)(2,1)} %param.32) | copy-start | bytes 786436
  96.5 286.5 %copy-start.17 = (s32[32]{0:T(128)S(1)}, s32[32]{0:T(128)}, u32[]{:S(2)}) copy-start(s32[32]{0:T(128)} %param.20) | copy-start | bytes 388
  96.5 287.1 %copy-start.18 = (s32[32]{0:T(128)S(1)}, s32[32]{0:T(128)}, u32[]{:S(2)}) copy-start(s32[32]{0:T(128)} %param.21) | copy-start | bytes 388
  96.5 424.7 %copy-start.15 = (f32[2048]{0:T(1024)S(1)}, f32[2048]{0:T(1024)}, u32[]{:S(2)}) copy-start(f32[2048]{0:T(1024)} %param.23) | copy-start | bytes 24580
  96.6 363.3 %all-gather.11.cloned.1.call-start = ((), (), s32[]{:S(2)}) async-start(), calls=%async_computation.8 | async-start | bytes 1179648 | tf_op jit(solution)/shard_map/all_gather | solution.py:106
  228.1 291.5 %all-gather.9.cloned.1.call-start = ((), (), s32[]{:S(2)}) async-start(), calls=%async_computation.5 | async-start | bytes 1179648 | tf_op jit(solution)/shard_map/all_gather | solution.py:106
  380.1 359.1 %all-gather.13.cloned.1.call-start = ((), (), s32[]{:S(2)}) async-start(), calls=%async_computation.10 | async-start | bytes 9437184 | tf_op jit(solution)/shard_map/all_gather | solution.py:134
  380.8 144.8 %collective-permute-start.1 = (bf16[1792,64]{0,1:T(8,128)(2,1)}, bf16[1792,64]{0,1:T(8,128)(2,1)S(1)}, u32[]{:S(2)}, u32[]{:S(2)}) collective-permute-start(bf16[1792,64]{0,1:T(8,128)(2,1)} %slice.35), channel_id=1, source_target_pairs={{0,8},{8,0},{16,24},{24,16},{32,40},{40,32},{48,56},{56,48},{64,72... | collective-permute-start | bytes 688136 | tf_op jit(solution)/shard_map/ppermute | solution.py:12
  382.5 180.5 %collective-permute-start = (bf16[1792,64]{0,1:T(8,128)(2,1)}, bf16[1792,64]{0,1:T(8,128)(2,1)}, u32[]{:S(2)}, u32[]{:S(2)}) collective-permute-start(bf16[1792,64]{0,1:T(8,128)(2,1)} %slice.33), channel_id=1, source_target_pairs={{0,8},{8,0},{16,24},{24,16},{32,40},{40,32},{48,56},{56,48},{64,72... | collective-permute-start | bytes 688136 | tf_op jit(solution)/shard_map/ppermute | solution.py:12
  519.6 4.0 copy-start.4
  519.6 4.0 copy-start.11
  521.3 3.1 copy-start.3
  521.3 3.1 copy-start.13
  533.8 29.2 %slice-start = ((s8[16777216]{0:T(1024)(128)(4,1)}), s8[4194304]{0:T(1024)(128)(4,1)S(1)}, s32[]{:S(2)}) async-start(s8[16777216]{0:T(1024)(128)(4,1)} %bitcast.176), calls=%async_computation.12 | async-start | bytes 8388608
  533.8 29.2 %slice-start.1 = ((s8[16777216]{0:T(1024)(128)(4,1)}), s8[4194304]{0:T(1024)(128)(4,1)S(1)}, s32[]{:S(2)}) async-start(s8[16777216]{0:T(1024)(128)(4,1)} %bitcast.176), calls=%async_computation.13 | async-start | bytes 8388608
  533.8 29.2 %slice-start.2 = ((s8[16777216]{0:T(1024)(128)(4,1)}), s8[4194304]{0:T(1024)(128)(4,1)S(1)}, s32[]{:S(2)}) async-start(s8[16777216]{0:T(1024)(128)(4,1)} %bitcast.176), calls=%async_computation.14 | async-start | bytes 8388608
  548.5 14.0 %copy-start.14 = (bf16[2048,64]{0,1:T(8,128)(2,1)S(1)}, bf16[2048,64]{0,1:T(8,128)(2,1)}, u32[]{:S(2)}) copy-start(bf16[2048,64]{0,1:T(8,128)(2,1)} %param.26) | copy-start | bytes 786436
  548.5 14.5 %slice-start.3 = ((s8[16777216]{0:T(1024)(128)(4,1)}), s8[4194304]{0:T(1024)(128)(4,1)S(1)}, s32[]{:S(2)}) async-start(s8[16777216]{0:T(1024)(128)(4,1)} %bitcast.176), calls=%async_computation.15 | async-start | bytes 8388608
  548.5 14.5 %copy-start.8 = (bf16[2048,64]{0,1:T(8,128)(2,1)S(1)}, bf16[2048,64]{0,1:T(8,128)(2,1)}, u32[]{:S(2)}) copy-start(bf16[2048,64]{0,1:T(8,128)(2,1)} %param.33) | copy-start | bytes 786436
  563.0 5.2 copy-start.1
  569.8 339.8 %all-gather.15.cloned.1.call-start = ((), (), s32[]{:S(2)}) async-start(), calls=%async_computation.11 | async-start | bytes 9437184 | tf_op jit(solution)/shard_map/all_gather | solution.py:134
  571.6 8.9 copy-start.2
  581.9 413.0 %reduce-scatter.7.cloned.1.call-start = ((), (), s32[]{:S(2)}) async-start(), calls=%async_computation.6 | async-start | bytes 1179648 | tf_op jit(solution)/shard_map/reduce_scatter | solution.py:144
  745.6 3.3 copy-start.9
  745.6 3.3 copy-start.16
  747.8 1.1 copy-start.5
  757.6 324.6 %reduce-scatter.11.cloned.1.call-start = ((), (), s32[]{:S(2)}) async-start(), calls=%async_computation.9 | async-start | bytes 1179648 | tf_op jit(solution)/shard_map/reduce_scatter | solution.py:144
  916.0 3.2 copy-start.10
  918.2 1.0 copy-start.6
  (1 other events, 0.9 us)
Sparse Core Ops, SparseCore 0:
  90.3 137.7 reduce-scatter.8
  230.6 149.4 reduce-scatter.4
  382.6 77.2 all-gather.10
  462.2 57.3 all-gather.8
  569.9 169.1 all-gather.12
  741.6 167.9 all-gather.14
  913.6 81.3 reduce-scatter.6
  999.4 82.7 reduce-scatter.10
